TPU v7x, 128 devices: a whole 4x4x4 slice. The times are simulated.
128 devices in a mesh: row: 16 (over z_lo, x, core), col: 8 (over y, z_hi).
Axes of the slice: x: 4, y: 4, z: 4 (z_hi: 2, z_lo: 2; z = z_hi * 2 + z_lo), core: 2. Of those that a mesh axis runs over, the one named last changes fastest.
Arguments:
- shared_rows: float32 [2048, 16384], P('row', 'col'), may hold values from -0.125 to 0.125
- event_counts: int32 [16], replicated, may hold values from 32 to 128, as said below
- ridge: float32 [16384], P('col'), may hold values from 0.5 to 2
- items: float32 [1024, 16384], P('row', 'col'), may hold values from -6 to 6
- cand_ids: int32 [512], replicated, may hold values from 0 to 1023
- theta: float32 [16384], P('col'), may hold values from -0.046875 to 0.046875
Outputs:
- gram_tile: float32 [16384, 16384], P('row', 'col')
- scores: float32 [512], replicated
Inputs may be any that keep to these rules, and one draw needn't show every extreme that they name: event_counts[s] counts the live slots at the start of row shard s's 128 slots; some shard is full.
All inputs are finite; a program needn't handle non-finite values.
Results may differ from a plain program's by a relative error of at most 0.000068.
Values sent between devices are 32-bit elements; how exact they have to be, the bound alone decides.
No kernel may reach another device: no remote copies, remote signals or barrier semaphores. Data moves between devices by JAX's collectives and lax.ppermute only.
A program may use at most 128 MiB of HBM per device.

v0:
```python
import jax
import jax.numpy as jnp
from jax import lax
from jax.sharding import PartitionSpec as P

F = 16384
high = lax.Precision.HIGHEST


def spread(value, axis, source):
    kept = jnp.where(lax.axis_index(axis) == source, value, 0).astype(value.dtype)
    return lax.psum(kept, axis)


def body(shared_rows, event_counts, ridge, items, cand_ids, theta):
    ratio = lax.axis_size("row") // lax.axis_size("col")
    row_pos = lax.axis_index("row")
    col_pos = lax.axis_index("col")
    width_col = shared_rows.shape[1]
    width_row = width_col // ratio
    ev_slots = shared_rows.shape[0]
    slot = lax.iota(jnp.int32, ev_slots)
    masked = jnp.where((slot < event_counts[row_pos])[:, None], shared_rows, jnp.float32(0.0))
    offset = row_pos % ratio * width_row
    root = row_pos // ratio
    contract = (((0,), (0,)), ((), ()))
    col_all = lax.all_gather(masked, "row", axis=0, tiled=True)
    row_all = spread(lax.dynamic_slice_in_dim(col_all, offset, width_row, 1), "col", root)
    tile = lax.dot_general(
        row_all, col_all, contract, precision=high, preferred_element_type=jnp.float32
    )
    rows_global = row_pos * width_row + lax.broadcasted_iota(jnp.int32, (width_row, width_col), 0)
    cols_global = col_pos * width_col + lax.broadcasted_iota(jnp.int32, (width_row, width_col), 1)
    tile = tile + jnp.where(rows_global == cols_global, ridge[None, :], jnp.float32(0.0))
    items_dev = items.shape[0]
    onehot = (
        cand_ids[:, None] == row_pos * items_dev + lax.iota(jnp.int32, items_dev)[None, :]
    ).astype(jnp.float32)
    picked = jnp.dot(onehot, items, precision=high, preferred_element_type=jnp.float32)
    cand_col = lax.psum(picked, "row")
    across = (((1,), (1,)), ((), ()))
    cand_row = spread(lax.dynamic_slice_in_dim(cand_col, offset, width_row, 1), "col", root)
    image_part = lax.dot_general(
        cand_col, tile, across, precision=high, preferred_element_type=jnp.float32
    )
    image_row = lax.psum(image_part, "col")
    quad = jnp.where(col_pos == 0, jnp.sum(cand_row * image_row, axis=1), jnp.float32(0.0))
    linear = jnp.where(
        row_pos == 0,
        jnp.dot(cand_col, theta, precision=high, preferred_element_type=jnp.float32),
        jnp.float32(0.0),
    )
    quad_all, linear_all = lax.psum((quad, linear), ("row", "col"))
    return (tile, linear_all + jnp.sqrt(quad_all / F))


def solution(mesh):
    return jax.shard_map(
        body,
        mesh=mesh,
        in_specs=(P("row", "col"), P(), P("col"), P("row", "col"), P(), P("col")),
        out_specs=(P("row", "col"), P()),
        check_vma=False,
    )
```

profile of v0, /device:TPU:1, one launch (start us, length us, event | category | flops | bytes accessed | tf_op | source)
XLA Modules:
  0.0 940.3 jit_solution(5957106584917055528)
XLA Ops:
  7.2 0.0 all-gather.2.cloned.1.call-start
  7.2 1.3 dynamic_slice.9
  8.5 0.6 iota_compare_fusion
  9.2 2.3 broadcast_select_fusion
  11.5 0.0 all-gather.2.cloned.1.call-update
  11.5 0.0 all-reduce.8.cloned.1.call-start
  11.6 4.5 fusion
  16.1 0.0 all-reduce.8.cloned.1.call-update
  16.1 0.0 all-reduce.6.cloned.1.call-start
  16.2 90.8 %all-gather.2.cloned.1.call-done = f32[2048,2048]{1,0:T(8,128)} async-done(((f32[128,2048]{1,0:T(8,128)}), f32[2048,2048]{1,0:T(8,128)}) %all-gather.2.cloned.1.call-update) | async-done | bytes 16777232 | tf_op jit(solution)/shard_map/all_gather | solution.py:27
  107.0 8.7 dynamic-slice_select_fusion
  115.7 0.0 all-reduce.10.cloned.1.call-start
  115.8 122.9 %all-reduce.8.cloned.1.call-done = f32[512,2048]{1,0:T(8,128)} async-done(((f32[512,2048]{1,0:T(8,128)}), f32[512,2048]{1,0:T(8,128)}) %all-reduce.8.cloned.1.call-update) | async-done | bytes 4194320 | tf_op jit(solution)/shard_map/psum | solution.py:40
  238.7 3.2 dynamic-slice_select_fusion.1
  241.9 343.4 %all-reduce.6.cloned.1.call-done = f32[2048,1024]{1,0:T(8,128)} async-done(((f32[2048,1024]{1,0:T(8,128)}), f32[2048,1024]{1,0:T(8,128)}) %all-reduce.6.cloned.1.call-update) | async-done | bytes 8388624 | tf_op jit(solution)/shard_map/psum | solution.py:12
  585.3 67.7 %select_add_fusion = f32[1024,2048]{1,0:T(8,128)S(1)} fusion(f32[2048]{0:T(1024)S(1)} %copy-done.3, s32[2048]{0:T(1024)S(1)} %iota_add_fusion, s32[1024]{0:T(1024)S(1)} %iota_add_fusion.1, f32[2048,1024]{1,0:T(8,128)} %all-reduce.6.cloned.1.call-done, f32[2048,2048]{1,0:T(8,128)} %all-gather.2.cloned.1.call-done), kind=kOutput, calls=%fused_computation | convolution fusion | flops 51545899008 | bytes 33574912 | tf_op jit(solution)/shard_map/dot_general | solution.py:29
  653.1 3.4 copy-done.4
  656.5 15.2 %fusion.5 = f32[512,1024]{1,0:T(8,128)} fusion(f32[512,2048]{1,0:T(8,128)S(1)} %copy-done.1, f32[1024,2048]{1,0:T(8,128)S(1)} %select_add_fusion), kind=kOutput, calls=%fused_computation.17 | convolution fusion | flops 12884901888 | bytes 14680064 | tf_op jit(solution)/shard_map/dot_general | solution.py:43
  671.7 0.0 all-reduce.10.cloned.1.call-update
  671.7 5.8 fusion.4
  677.5 185.2 %all-reduce.10.cloned.1.call-done = (f32[512,1024]{1,0:T(8,128)}, f32[512,1024]{1,0:T(8,128)}) async-done(((f32[512,1024]{1,0:T(8,128)}, f32[512,1024]{1,0:T(8,128)}), (f32[512,1024]{1,0:T(8,128)}, f32[512,1024]{1,0:T(8,128)})) %all-reduce.10.cloned.1.call-update) | async-done | bytes 4194320 | tf_op jit(solution)/shard_map/psum | solution.py:12
  862.7 2.5 multiply_reduce_fusion
  865.2 67.8 %all-reduce = (f32[512]{0:T(512)S(1)}, f32[512]{0:T(512)S(1)}) all-reduce(f32[512]{0:T(512)S(1)} %broadcast_select_fusion.2, f32[512]{0:T(512)S(1)} %broadcast_select_fusion.1), channel_id=1, replica_groups=mesh['row'=16,'col'=8] {'row','col'}, use_global_device_ids=true, to_apply=%region_2.3 | all-reduce | flops 1024 | bytes 8192 | tf_op jit(solution)/shard_map/psum | solution.py:53
  933.0 0.6 sqrt_add_fusion
  (15 shorter events, 0.1 us)
Async XLA Ops:
  7.2 4.4 copy-start
  7.2 99.8 %all-gather.2.cloned.1.call-start = ((), (), s32[]{:S(2)}) async-start(), calls=%async_computation | async-start | bytes 17825792 | tf_op jit(solution)/shard_map/all_gather | solution.py:27
  11.5 227.2 %all-reduce.8.cloned.1.call-start = ((), (), s32[]{:S(2)}) async-start(), calls=%async_computation.2 | async-start | bytes 8388608 | tf_op jit(solution)/shard_map/psum | solution.py:40
  16.1 569.2 %all-reduce.6.cloned.1.call-start = ((), (), s32[]{:S(2)}) async-start(), calls=%async_computation.1 | async-start | bytes 16777216 | tf_op jit(solution)/shard_map/psum | solution.py:12
  115.7 469.7 %copy-start.3 = (f32[2048]{0:T(1024)S(1)}, f32[2048]{0:T(1024)}, u32[]{:S(2)}) copy-start(f32[2048]{0:T(1024)} %param.8) | copy-start | bytes 24580
  115.7 747.0 %all-reduce.10.cloned.1.call-start = ((), (), s32[]{:S(2)}) async-start(), calls=%async_computation.3 | async-start | bytes 8388608 | tf_op jit(solution)/shard_map/psum | solution.py:12
  585.3 71.1 %copy-start.1 = (f32[512,2048]{1,0:T(8,128)S(1)}, f32[512,2048]{1,0:T(8,128)}, u32[]{:S(2)}) copy-start(f32[512,2048]{1,0:T(8,128)} %all-reduce.8.cloned.1.call-done) | copy-start | bytes 12582916
  653.1 3.4 copy-start.4
  656.5 15.3 %copy-start.2 = (f32[2048]{0:T(1024)S(1)}, f32[2048]{0:T(1024)}, u32[]{:S(2)}) copy-start(f32[2048]{0:T(1024)} %param.11) | copy-start | bytes 24580
Sparse Core Ops, SparseCore 0:
  11.7 95.2 all-gather.1
  109.5 129.1 all-reduce.7
  241.8 343.4 all-reduce.5
  671.8 190.8 all-reduce.9
where the time goes:
time: 944 us; the launch traced here: 940 us
  waiting for transfers between devices  742 us (79%)
  matrix products  93.2 us (10%)
  blocking collectives  67.8 us (7%)
  other arithmetic  18 us (2%)
  between operations  14.1 us (1%)
    psum x2, waiting for transfers between devices, spread(): return lax.psum(kept, axis)  529 us
    psum x1, waiting for transfers between devices, body(): cand_col = lax.psum(picked, 'row')  123 us
    all_gather x1, waiting for transfers between devices, body(): col_all = lax.all_gather(masked, 'row', axis=0, tiled=True)  90.8 us
    psum x1, blocking collectives, body(): quad_all, linear_all = lax.psum((quad, linear), ('row', 'col'))  67.8 us
    dot_general x1, matrix products, body(): lax.dot_general(row_all, col_all, contract, precision=high, preferred_ele...  67.7 us
  transfers between devices with their start and end apart: 4, of which 4 were waited for; matrix products, arithmetic and copies ran while one was open for 2% of the time, Pallas kernels for 0%

commit v1 on v0

--- a/solution.py
+++ b/solution.py
@@ -5,6 +5,12 @@
 
 F = 16384
 high = lax.Precision.HIGHEST
+
+
+def gather_and_add(x, axis):
+    pieces = lax.all_gather(x, axis, axis=0, tiled=False)
+    total = pieces.sum(axis=0)
+    return total
 
 
 def spread(value, axis, source):
@@ -37,7 +43,7 @@
         cand_ids[:, None] == row_pos * items_dev + lax.iota(jnp.int32, items_dev)[None, :]
     ).astype(jnp.float32)
     picked = jnp.dot(onehot, items, precision=high, preferred_element_type=jnp.float32)
-    cand_col = lax.psum(picked, "row")
+    cand_col = gather_and_add(picked, "row")
     across = (((1,), (1,)), ((), ()))
     cand_row = spread(lax.dynamic_slice_in_dim(cand_col, offset, width_row, 1), "col", root)
     image_part = lax.dot_general(

time: 944 us -> 1100 us (1.17)
  waiting for transfers between devices: 742 us -> 890 us
  other arithmetic: 18 us -> 40.9 us
    all_gather x0 -> x1, waiting for transfers between devices: none -> 276 us  [gather_and_add(): pieces = lax.all_gather(x, axis, axis=0, tiled=False)]
    psum x1 -> x0, waiting for transfers between devices: 123 us -> none  [body(): cand_col = lax.psum(picked, 'row')]
    reduce_sum x0 -> x1, other arithmetic: none -> 22.9 us  [gather_and_add(): total = pieces.sum(axis=0)]
  transfers between devices with their start and end apart: 4 -> 4, of which waited for: 4 -> 4; matrix products, arithmetic and copies ran while one was open for 2% -> 6% of each run, Pallas kernels for 0% -> 0%
where the time goes in v1:
time: 1100 us
  waiting for transfers between devices  890 us (81%)
  matrix products  86.9 us (8%)
  blocking collectives  67.8 us (6%)
  other arithmetic  40.9 us (4%)
  between operations  13.9 us (1%)
    psum x2, waiting for transfers between devices, spread(): return lax.psum(kept, axis)  519 us
    all_gather x1, waiting for transfers between devices, gather_and_add(): pieces = lax.all_gather(x, axis, axis=0, tiled=False)  276 us
    all_gather x1, waiting for transfers between devices, body(): col_all = lax.all_gather(masked, 'row', axis=0, tiled=True)  95.4 us
    psum x1, blocking collectives, body(): quad_all, linear_all = lax.psum((quad, linear), ('row', 'col'))  67.8 us
    dot_general x1, matrix products, body(): lax.dot_general(row_all, col_all, contract, precision=high, preferred_ele...  59.7 us
    reduce_sum x1, other arithmetic, gather_and_add(): total = pieces.sum(axis=0)  22.9 us
  transfers between devices with their start and end apart: 4, of which 4 were waited for; matrix products, arithmetic and copies ran while one was open for 6% of the time, Pallas kernels for 0%

profile of v1, /device:TPU:1, one launch (start us, length us, event | category | flops | bytes accessed | tf_op | source)
XLA Modules:
  0.0 1101.5 jit_solution(2486135744850171027)
XLA Ops:
  7.2 0.0 all-gather.4.cloned.1.call-start
  7.2 1.3 dynamic_slice.9
  8.5 0.6 iota_compare_fusion
  9.2 2.3 broadcast_select_fusion
  11.5 0.0 all-gather.4.cloned.1.call-update
  11.5 0.0 all-reduce.5.cloned.1.call-start
  11.6 95.4 %all-gather.4.cloned.1.call-done = f32[2048,2048]{1,0:T(8,128)} async-done(((f32[128,2048]{1,0:T(8,128)}), f32[2048,2048]{1,0:T(8,128)}) %all-gather.4.cloned.1.call-update) | async-done | bytes 16777232 | tf_op jit(solution)/shard_map/all_gather | solution.py:33
  107.0 8.7 dynamic-slice_select_fusion
  115.7 0.0 all-gather.6.cloned.1.call-start
  115.8 0.6 copy-done.2
  116.3 3.8 fusion
  120.2 0.0 all-reduce.7.cloned.1.call-start
  120.3 338.0 %all-reduce.5.cloned.1.call-done = f32[2048,1024]{1,0:T(8,128)} async-done(((f32[2048,1024]{1,0:T(8,128)}), f32[2048,1024]{1,0:T(8,128)}) %all-reduce.5.cloned.1.call-update) | async-done | bytes 8388624 | tf_op jit(solution)/shard_map/psum | solution.py:18
  458.2 59.7 %select_add_fusion = f32[1024,2048]{1,0:T(8,128)} fusion(f32[2048]{0:T(1024)S(1)} %copy-done.3, s32[2048]{0:T(1024)S(1)} %iota_add_fusion, s32[1024]{0:T(1024)S(1)} %iota_add_fusion.1, f32[2048,1024]{1,0:T(8,128)} %all-reduce.5.cloned.1.call-done, f32[2048,2048]{1,0:T(8,128)} %all-gather.4.cloned.1.call-done), kind=kOutput, calls=%fused_computation | convolution fusion | flops 51545899008 | bytes 33574912 | tf_op jit(solution)/shard_map/dot_general | solution.py:35
  518.0 275.6 %all-gather.6.cloned.1.call-done = f32[8192,2048]{1,0:T(8,128)} async-done(((f32[512,2048]{1,0:T(8,128)}), f32[8192,2048]{1,0:T(8,128)}) %all-gather.6.cloned.1.call-update) | async-done | bytes 67108880 | tf_op jit(solution)/shard_map/all_gather | solution.py:11
  793.6 22.9 %reduce_sum.18 = f32[512,2048]{1,0:T(8,128)} reduce(f32[16,512,2048]{2,1,0:T(8,128)} %bitcast.1, f32[]{:T(128)} %constant.42.clone.1), dimensions={0}, to_apply=%region_1.2 | reduce | flops 15728640 | bytes 71303168 | tf_op jit(solution)/shard_map/reduce_sum | solution.py:12
  816.5 3.2 dynamic-slice_select_fusion.1
  819.7 17.6 %fusion.5 = f32[512,1024]{1,0:T(8,128)} fusion(f32[512,2048]{1,0:T(8,128)} %reduce_sum.18, f32[1024,2048]{1,0:T(8,128)} %select_add_fusion), kind=kOutput, calls=%fused_computation.17 | convolution fusion | flops 12884901888 | bytes 14680064 | tf_op jit(solution)/shard_map/dot_general | solution.py:49
  837.3 0.0 all-reduce.7.cloned.1.call-update
  837.3 5.8 fusion.4
  843.1 181.0 %all-reduce.7.cloned.1.call-done = (f32[512,1024]{1,0:T(8,128)}, f32[512,1024]{1,0:T(8,128)}) async-done(((f32[512,1024]{1,0:T(8,128)}, f32[512,1024]{1,0:T(8,128)}), (f32[512,1024]{1,0:T(8,128)}, f32[512,1024]{1,0:T(8,128)})) %all-reduce.7.cloned.1.call-update) | async-done | bytes 4194320 | tf_op jit(solution)/shard_map/psum | solution.py:18
  1024.0 2.5 multiply_reduce_fusion
  1026.5 67.8 %all-reduce = (f32[512]{0:T(512)S(1)}, f32[512]{0:T(512)S(1)}) all-reduce(f32[512]{0:T(512)S(1)} %broadcast_select_fusion.2, f32[512]{0:T(512)S(1)} %broadcast_select_fusion.1), channel_id=1, replica_groups=mesh['row'=16,'col'=8] {'row','col'}, use_global_device_ids=true, to_apply=%region_2.3 | all-reduce | flops 1024 | bytes 8192 | tf_op jit(solution)/shard_map/psum | solution.py:59
  1094.3 0.6 sqrt_add_fusion
  (14 shorter events, 0.1 us)
Async XLA Ops:
  7.2 108.6 %copy-start = (f32[64,2048]{1,0:T(8,128)S(1)}, f32[64,2048]{1,0:T(8,128)}, u32[]{:S(2)}) copy-start(f32[64,2048]{1,0:T(8,128)} %param.9) | copy-start | bytes 1572868
  7.2 99.8 %all-gather.4.cloned.1.call-start = ((), (), s32[]{:S(2)}) async-start(), calls=%async_computation | async-start | bytes 17825792 | tf_op jit(solution)/shard_map/all_gather | solution.py:33
  11.5 446.7 %all-reduce.5.cloned.1.call-start = ((), (), s32[]{:S(2)}) async-start(), calls=%async_computation.1 | async-start | bytes 16777216 | tf_op jit(solution)/shard_map/psum | solution.py:18
  115.7 0.7 copy-start.2
  115.7 342.6 %copy-start.3 = (f32[2048]{0:T(1024)S(1)}, f32[2048]{0:T(1024)}, u32[]{:S(2)}) copy-start(f32[2048]{0:T(1024)} %param.8) | copy-start | bytes 24580
  115.7 677.9 %all-gather.6.cloned.1.call-start = ((), (), s32[]{:S(2)}) async-start(), calls=%async_computation.2 | async-start | bytes 71303168 | tf_op jit(solution)/shard_map/all_gather | solution.py:11
  120.2 903.9 %all-reduce.7.cloned.1.call-start = ((), (), s32[]{:S(2)}) async-start(), calls=%async_computation.3 | async-start | bytes 8388608 | tf_op jit(solution)/shard_map/psum | solution.py:18
  819.7 17.6 %copy-start.1 = (f32[2048]{0:T(1024)S(1)}, f32[2048]{0:T(1024)}, u32[]{:S(2)}) copy-start(f32[2048]{0:T(1024)} %param.11) | copy-start | bytes 24580
Sparse Core Ops, SparseCore 0:
  11.7 95.2 all-gather.3
  115.8 342.3 all-reduce.4
  459.9 333.5 all-gather.5
  837.4 186.5 all-reduce.6
